TPU v7x, 512 devices: a whole 4x8x8 slice. The times are simulated.
512 devices in a mesh: req: 64 (over x, z, core), ch: 8 (over y).
Axes of the slice: x: 4, y: 8, z: 8, core: 2. Of those that a mesh axis runs over, the one named last changes fastest.
Arguments:
- tokens: bfloat16 [128, 4096], P('req', 'ch'), may hold values from -80 to 80
- attn_gain: float32 [4096], P('ch'), may hold values from 0.1 to 1.9
- w_query: bfloat16 [4096, 4096], P('ch', 'req'), may hold values from -0.09375 to 0.09375
- w_keyval: bfloat16 [4096, 512], P('ch', 'req'), may hold values from -0.09375 to 0.09375
- cache: bfloat16 [2, 128, 256, 2048], P(None, 'req', 'ch'), may hold values from -70 to 70
- lengths: int32 [128], P('req'), may hold values from 1 to 2047, as said below
- write_pos: int32 [128], P('req'), may hold values from 0 to 2047
- w_out: bfloat16 [4096, 4096], P('ch', 'req'), may hold values from -0.09375 to 0.09375
- mlp_gain: float32 [4096], P('ch'), may hold values from 0.1 to 1.9
- w_gate_up: bfloat16 [4096, 24576], P('ch', 'req'), may hold values from -0.09375 to 0.09375
- w_down: bfloat16 [12288, 4096], P('req', 'ch'), may hold values from -0.0546875 to 0.0546875
Outputs:
- layer_out: bfloat16 [128, 4096], P('req', 'ch')
- kv_new: bfloat16 [128, 512], P('req', 'ch')
Inputs may be any that keep to these rules, and one draw needn't show every extreme that they name: lengths[b] earlier tokens of request b are in the cache; the largest equals 2047 in every draw. The new token of request b goes to slot write_pos[b]; its earlier tokens fill the slots before it, going back cyclically.
All inputs are finite; a program needn't handle non-finite values.
Results may differ from a plain program's by a relative error of at most 0.0064.
Values may be sent and summed in bfloat16 or wider, within the bound.
No kernel may reach another device: no remote copies, remote signals or barrier semaphores. Data moves between devices by JAX's collectives and lax.ppermute only.
A program may use at most 64 MiB of HBM per device.

v0:
```python
import math
import jax
import jax.numpy as jnp
from jax import lax
from jax.sharding import PartitionSpec as P

D = 4096
H = 16
HD = 256
EPSILON = 1e-06


def rms_norm(values, gain):
    wide = values.astype(jnp.float32)
    squares = jnp.sum(wide * wide, axis=1)
    summed = lax.psum(squares, "ch")
    meansq = summed / D
    return (wide * lax.rsqrt(meansq + EPSILON)[:, None] * gain[None, :]).astype(jnp.bfloat16)


def body(
    tokens,
    attn_gain,
    w_query,
    w_keyval,
    cache,
    lengths,
    write_pos,
    w_out,
    mlp_gain,
    w_gate_up,
    w_down,
):
    rows = tokens.shape[0]
    chan = cache.shape[2]
    window = cache.shape[3]
    factor = 1.0 / math.sqrt(HD)
    normed = rms_norm(tokens, attn_gain)
    joined = jnp.concatenate([w_query, w_keyval], axis=1)
    head_parts = jnp.dot(
        lax.all_gather(normed, "req", axis=0, tiled=True),
        joined,
        preferred_element_type=jnp.float32,
    )
    query_cols = w_query.shape[1]
    query_part, keyval_part = (
        lax.all_to_all(head_parts[:, :query_cols], "req", split_axis=0, concat_axis=1, tiled=True),
        lax.all_to_all(head_parts[:, query_cols:], "req", split_axis=0, concat_axis=1, tiled=True),
    )
    query_sum, keyval_sum = (
        lax.psum_scatter(query_part, "ch", scatter_dimension=1, tiled=True),
        lax.psum_scatter(keyval_part, "ch", scatter_dimension=1, tiled=True),
    )
    queries = query_sum.astype(jnp.bfloat16).reshape(rows, H, chan)
    keyval_new = keyval_sum.astype(jnp.bfloat16)
    key_new = keyval_new[:, :chan]
    value_new = keyval_new[:, chan:]
    keys = cache[0]
    values_cache = cache[1]
    own_part = jnp.sum(
        queries.astype(jnp.float32) * key_new.astype(jnp.float32)[:, None, :], axis=-1
    )
    score_part = jnp.einsum("bhe,bew->bhw", queries, keys, preferred_element_type=jnp.float32)
    summed, own_sum = lax.psum((score_part, own_part), "ch")
    slot_index = jnp.arange(window, dtype=jnp.int32)
    offset = (write_pos[:, None] - 1 - slot_index[None, :]) % window
    usable = offset < lengths[:, None]
    scores = jnp.where(usable[:, None, :], summed * factor, -jnp.inf)
    own_score = own_sum * factor
    top = jnp.maximum(jnp.max(scores, axis=-1), own_score)
    weights = jnp.exp(scores - top[..., None])
    own_weight = jnp.exp(own_score - top)
    total = jnp.sum(weights, axis=-1) + own_weight
    weights_low = weights.astype(jnp.bfloat16)
    numer = jnp.einsum(
        "bhw,bew->bhe", weights_low, values_cache, preferred_element_type=jnp.float32
    )
    numer = (
        numer
        + own_weight.astype(jnp.bfloat16).astype(jnp.float32)[..., None]
        * value_new.astype(jnp.float32)[:, None, :]
    )
    attn_local = (numer / total[..., None]).astype(jnp.bfloat16).reshape(rows, H * chan)
    out_parts = jnp.dot(
        lax.all_gather(attn_local, "req", axis=0, tiled=True),
        w_out,
        preferred_element_type=jnp.float32,
    )
    out_part = lax.all_to_all(out_parts, "req", split_axis=0, concat_axis=1, tiled=True)
    out_sum = lax.psum_scatter(out_part, "ch", scatter_dimension=1, tiled=True)
    first = (tokens.astype(jnp.float32) + out_sum).astype(jnp.bfloat16)
    normed_two = rms_norm(first, mlp_gain)
    hidden_cols = w_gate_up.shape[1] // 2
    ffn_parts = jnp.dot(
        lax.all_gather(normed_two, "req", axis=0, tiled=True),
        w_gate_up,
        preferred_element_type=jnp.float32,
    )
    ffn_total = lax.psum(ffn_parts, "ch")
    hidden = (
        jax.nn.gelu(ffn_total[:, :hidden_cols], approximate=True) * ffn_total[:, hidden_cols:]
    ).astype(jnp.bfloat16)
    down_sum = lax.psum_scatter(
        jnp.dot(hidden, w_down, preferred_element_type=jnp.float32),
        "req",
        scatter_dimension=0,
        tiled=True,
    )
    layer_out = (first.astype(jnp.float32) + down_sum).astype(jnp.bfloat16)
    return (layer_out, keyval_new)


def solution(mesh):
    placed = (
        P("req", "ch"),
        P("ch"),
        P("ch", "req"),
        P("ch", "req"),
        P(None, "req", "ch", None),
        P("req"),
        P("req"),
        P("ch", "req"),
        P("ch"),
        P("ch", "req"),
        P("req", "ch"),
    )
    return jax.shard_map(
        body,
        mesh=mesh,
        in_specs=placed,
        out_specs=(P("req", "ch"), P("req", "ch")),
        check_vma=False,
    )
```

profile of v0, /device:TPU:1, one launch (start us, length us, event | category | flops | bytes accessed | tf_op | source)
XLA Modules:
  0.0 728.1 jit_solution(11447148937282177522)
XLA Ops:
  7.2 0.8 fusion.36
  8.0 14.7 %psum.35 = f32[2]{0:T(128)S(1)} all-reduce(f32[2]{0:T(128)S(1)} %fusion.36), channel_id=1, replica_groups=mesh['req'=64,'ch'=8] {'ch'}, use_global_device_ids=true, to_apply=%region_1.0 | all-reduce | flops 2 | bytes 16 | tf_op jit(solution)/shard_map/psum | solution.py:16
  22.7 0.8 fusion.45
  23.5 60.2 %all-gather = bf16[64,2,512]{2,1,0:T(2,128)(2,1)S(1)} all-gather(bf16[1,2,512]{2,1,0:T(2,128)(2,1)S(1)} %fusion.45), channel_id=1, replica_groups=mesh['req'=64,'ch'=8] {'req'}, dimensions={0}, use_global_device_ids=true | all-gather | bytes 133120 | tf_op jit(solution)/shard_map/all_gather | solution.py:41
  83.7 0.1 reshape.72
  83.7 1.0 fusion.24
  84.8 0.7 copy.28
  85.5 5.6 all-to-all-start.1
  91.1 0.1 copy.26
  91.2 0.7 reshape.85
  91.9 8.9 %all-to-all-done.1 = f32[64,2,8]{2,1,0:T(2,128)S(1)} async-done(((f32[64,2,8]{2,1,0:T(2,128)}), f32[64,2,8]{2,1,0:T(2,128)S(1)}, u32[]{:S(2)}, u32[]{:S(2)}) %all-to-all-start.1) | async-done | bytes 4128 | tf_op jit(solution)/shard_map/all_to_all | solution.py:48
  100.8 4.4 all-to-all-start
  105.2 0.0 reduce-scatter.12.cloned.1.call-start
  105.2 1.2 copy.40
  106.4 0.0 reduce-scatter.12.cloned.1.call-update
  106.4 0.0 reduce-scatter.10.cloned.1.call-start
  106.5 0.7 broadcast_add_fusion
  107.2 7.5 %all-to-all-done = f32[64,1,128]{2,1,0:T(1,128)S(1)} async-done(((f32[64,1,128]{2,1,0:T(1,128)}), f32[64,1,128]{2,1,0:T(1,128)S(1)}, u32[]{:S(2)}, u32[]{:S(2)}) %all-to-all-start) | async-done | bytes 32800 | tf_op jit(solution)/shard_map/all_to_all | solution.py:47
  114.6 0.5 broadcast.73
  115.1 0.7 reduce
  115.9 0.1 reshape.86
  116.0 2.0 copy.39
  118.0 0.0 reduce-scatter.10.cloned.1.call-update
  118.1 0.0 all-reduce.5.cloned.1.call-start
  118.1 0.1 fusion.35
  118.2 23.1 %reduce-scatter.12.cloned.1.call-done = f32[64,2]{1,0:T(8,128)} async-done(((f32[512,2]{1,0:T(8,128)}), f32[64,2]{1,0:T(8,128)}) %reduce-scatter.12.cloned.1.call-update) | async-done | bytes 528
  141.3 0.8 copy.36
  142.2 47.1 %reduce-scatter.10.cloned.1.call-done = f32[512,2]{1,0:T(8,128)} async-done(((f32[4096,2]{1,0:T(8,128)}), f32[512,2]{1,0:T(8,128)}) %reduce-scatter.10.cloned.1.call-update) | async-done | bytes 4112
  189.3 1.1 copy.34
  190.4 0.1 reshape.69
  190.5 0.9 fusion.3
  191.4 0.0 reduce-scatter.14.cloned.1.call-start
  191.4 0.1 slice_convert_fusion
  191.5 0.1 multiply_reduce_fusion
  191.6 11.9 %psum.37 = f32[2,16]{1,0:T(2,128)S(1)} all-reduce(f32[2,16]{1,0:T(2,128)S(1)} %multiply_reduce_fusion), channel_id=1, replica_groups=mesh['req'=64,'ch'=8] {'ch'}, use_global_device_ids=true, to_apply=%region_7.8 | all-reduce | flops 32 | bytes 256 | tf_op jit(solution)/shard_map/psum | solution.py:64
  203.5 64.4 %all-reduce.5.cloned.1.call-done = f32[2,16,2048]{2,1,0:T(8,128)} async-done(((f32[2,16,2048]{2,1,0:T(8,128)}), f32[2,16,2048]{2,1,0:T(8,128)}) %all-reduce.5.cloned.1.call-update) | async-done | bytes 262160 | tf_op jit(solution)/shard_map/psum | solution.py:64
  267.9 1.1 fusion.7
  269.0 1.2 fusion.8
  270.1 1.2 fusion.1
  271.4 0.1 reshape.73
  271.4 57.0 %all-gather.1 = bf16[64,2,512]{2,1,0:T(2,128)(2,1)S(1)} all-gather(bf16[1,2,512]{2,1,0:T(2,128)(2,1)S(1)} %reshape.73), channel_id=1, replica_groups=mesh['req'=64,'ch'=8] {'req'}, dimensions={0}, use_global_device_ids=true | all-gather | bytes 133120 | tf_op jit(solution)/shard_map/all_gather | solution.py:85
  328.4 0.1 reshape.74
  328.5 0.2 fusion.55
  328.7 0.1 reshape.87
  328.8 16.1 %all_to_all.57 = f32[64,1,128]{2,1,0:T(1,128)S(1)} all-to-all(f32[64,1,128]{2,1,0:T(1,128)S(1)} %reshape.87), channel_id=1, replica_groups=mesh['req'=64,'ch'=8] {'req'}, dimensions={0} | all-to-all | bytes 65536 | tf_op jit(solution)/shard_map/all_to_all | solution.py:89
  344.9 0.7 reduce.1
  345.6 0.1 reshape.88
  345.8 2.0 copy.41
  347.8 0.0 reduce-scatter.14.cloned.1.call-update
  347.8 0.0 all-reduce.7.cloned.1.call-start
  347.9 32.4 %reduce-scatter.14.cloned.1.call-done = f32[512,2]{1,0:T(8,128)} async-done(((f32[4096,2]{1,0:T(8,128)}), f32[512,2]{1,0:T(8,128)}) %reduce-scatter.14.cloned.1.call-update) | async-done | bytes 4112
  380.3 1.1 copy.38
  381.4 0.1 fusion.40
  381.5 12.0 %psum.38 = f32[2]{0:T(128)S(1)} all-reduce(f32[2]{0:T(128)S(1)} %get-tuple-element.2), channel_id=1, replica_groups=mesh['req'=64,'ch'=8] {'ch'}, use_global_device_ids=true, to_apply=%region_11.12 | all-reduce | flops 2 | bytes 16 | tf_op jit(solution)/shard_map/psum | solution.py:16
  393.5 0.1 fusion.44
  393.6 59.6 %all-gather.2 = bf16[64,2,512]{2,1,0:T(2,128)(2,1)S(1)} all-gather(bf16[1,2,512]{2,1,0:T(2,128)(2,1)S(1)} %fusion.44), channel_id=1, replica_groups=mesh['req'=64,'ch'=8] {'req'}, dimensions={0}, use_global_device_ids=true | all-gather | bytes 133120 | tf_op jit(solution)/shard_map/all_gather | solution.py:95
  453.2 0.1 reshape.76
  453.2 0.9 fusion.56
  454.2 0.0 all-reduce.9.cloned.1.call-start
  454.2 69.2 %all-reduce.7.cloned.1.call-done = f32[128,384]{1,0:T(8,128)} async-done(((f32[128,384]{1,0:T(8,128)}), f32[128,384]{1,0:T(8,128)}) %all-reduce.7.cloned.1.call-update) | async-done | bytes 196624 | tf_op jit(solution)/shard_map/psum | solution.py:99
  523.4 1.9 fusion.28
  525.3 1.3 dynamic-slice
  527.3 192.7 %all-reduce.9.cloned.1.call-done = f32[128,512]{1,0:T(8,128)} async-done(((f32[128,512]{1,0:T(8,128)}), f32[128,512]{1,0:T(8,128)}) %all-reduce.9.cloned.1.call-update) | async-done | bytes 262160
  720.0 1.3 fusion.43
  (25 shorter events, 0.1 us)
Async XLA Ops:
  7.2 446.1 %copy-start = (bf16[512,384]{1,0:T(8,128)(2,1)S(1)}, bf16[512,384]{1,0:T(8,128)(2,1)}, u32[]{:S(2)}) copy-start(bf16[512,384]{1,0:T(8,128)(2,1)} %param.20) | copy-start | bytes 1179652
  85.5 15.3 %all-to-all-start.1 = ((f32[64,2,8]{2,1,0:T(2,128)}), f32[64,2,8]{2,1,0:T(2,128)S(1)}, u32[]{:S(2)}, u32[]{:S(2)}) async-start(f32[64,2,8]{2,1,0:T(2,128)} %bitcast.4), calls=%async_computation.1 | async-start | bytes 131072 | tf_op jit(solution)/shard_map/all_to_all | solution.py:48
  100.8 13.8 %all-to-all-start = ((f32[64,1,128]{2,1,0:T(1,128)}), f32[64,1,128]{2,1,0:T(1,128)S(1)}, u32[]{:S(2)}, u32[]{:S(2)}) async-start(f32[64,1,128]{2,1,0:T(1,128)} %reshape.85), calls=%async_computation | async-start | bytes 65536 | tf_op jit(solution)/shard_map/all_to_all | solution.py:47
  105.2 36.1 %reduce-scatter.12.cloned.1.call-start = ((), (), s32[]{:S(2)}) async-start(), calls=%async_computation.9 | async-start | bytes 294912
  106.4 82.9 %reduce-scatter.10.cloned.1.call-start = ((), (), s32[]{:S(2)}) async-start(), calls=%async_computation.8 | async-start | bytes 2359296
  116.0 2.2 copy-start.7
  116.0 74.5 %copy-start.2 = (bf16[2,2,32,2048]{3,2,1,0:T(8,128)(2,1)S(1)}, bf16[2,2,32,2048]{3,2,1,0:T(8,128)(2,1)}, u32[]{:S(2)}) copy-start(bf16[2,2,32,2048]{3,2,1,0:T(8,128)(2,1)} %param.15) | copy-start | bytes 1572868
  118.0 210.5 %copy-start.3 = (bf16[512,64]{0,1:T(8,128)(2,1)S(1)}, bf16[512,64]{0,1:T(8,128)(2,1)}, u32[]{:S(2)}) copy-start(bf16[512,64]{0,1:T(8,128)(2,1)} %param.18) | copy-start | bytes 196612
  118.1 149.8 %all-reduce.5.cloned.1.call-start = ((), (), s32[]{:S(2)}) async-start(), calls=%async_computation.6 | async-start | bytes 524288 | tf_op jit(solution)/shard_map/psum | solution.py:64
  142.2 205.6 %copy-start.5 = (bf16[2,64]{1,0:T(2,128)(2,1)}, bf16[2,64]{1,0:T(2,128)(2,1)S(1)}, u32[]{:S(2)}) copy-start(bf16[2,64]{1,0:T(2,128)(2,1)S(1)} %copy.36) | copy-start | bytes 772
  191.4 188.9 %reduce-scatter.14.cloned.1.call-start = ((), (), s32[]{:S(2)}) async-start(), calls=%async_computation.10 | async-start | bytes 2359296
  345.7 35.6 %copy-start.4 = (bf16[2,512]{1,0:T(2,128)(2,1)S(1)}, bf16[2,512]{1,0:T(2,128)(2,1)}, u32[]{:S(2)}) copy-start(bf16[2,512]{1,0:T(2,128)(2,1)} %param.11) | copy-start | bytes 6148
  345.8 47.8 %copy-start.6 = (f32[512]{0:T(512)S(1)}, f32[512]{0:T(512)}, u32[]{:S(2)}) copy-start(f32[512]{0:T(512)} %param.19) | copy-start | bytes 6148
  347.8 175.6 %copy-start.1 = (bf16[192,512]{1,0:T(8,128)(2,1)S(1)}, bf16[192,512]{1,0:T(8,128)(2,1)}, u32[]{:S(2)}) copy-start(bf16[192,512]{1,0:T(8,128)(2,1)} %param.21) | copy-start | bytes 589828
  347.8 175.6 %all-reduce.7.cloned.1.call-start = ((), (), s32[]{:S(2)}) async-start(), calls=%async_computation.7 | async-start | bytes 393216 | tf_op jit(solution)/shard_map/psum | solution.py:99
  454.2 265.8 %all-reduce.9.cloned.1.call-start = ((), (), s32[]{:S(2)}) async-start(), calls=%async_computation.11 | async-start | bytes 524288
Sparse Core Ops, SparseCore 0:
  108.8 32.4 reduce-scatter.11
  144.2 45.0 reduce-scatter.9
  191.6 76.2 all-reduce.4
  348.0 32.2 reduce-scatter.13
  454.3 69.0 all-reduce.6
  526.7 193.2 all-reduce.8
where the time goes:
time: 729 us; the launch traced here: 728 us
  waiting for transfers between devices  446 us (61%)
  blocking collectives  231 us (32%)
  between operations  15 us (2%)
  local copies, waits for them, and re-layouts  12.2 us (2%)
  starting transfers between devices  10.2 us (1%)
  other arithmetic  7.74 us (1%)
    unnamed x10, waiting for transfers between devices  295 us
    psum x1, waiting for transfers between devices, body(): ffn_total = lax.psum(ffn_parts, 'ch')  69.2 us
    psum x1, waiting for transfers between devices, body(): summed, own_sum = lax.psum((score_part, own_part), 'ch')  64.4 us
    all_gather x1, blocking collectives, body(): lax.all_gather(normed, 'req', axis=0, tiled=True)  60.2 us
    all_gather x1, blocking collectives, body(): lax.all_gather(normed_two, 'req', axis=0, tiled=True)  59.6 us
    all_gather x1, blocking collectives, body(): lax.all_gather(attn_local, 'req', axis=0, tiled=True)  57 us
    psum x2, blocking collectives, rms_norm(): summed = lax.psum(squares, 'ch')  26.7 us
    all_to_all x1, blocking collectives, body(): lax.all_to_all(out_parts, 'req', split_axis=0, concat_axis=1, tiled=True)  16.1 us
  transfers between devices with their start and end apart: 8, of which 8 were waited for; matrix products, arithmetic and copies ran while one was open for 1% of the time, Pallas kernels for 0%

commit v1 on v0

--- a/solution.py
+++ b/solution.py
@@ -8,6 +8,11 @@
 H = 16
 HD = 256
 EPSILON = 1e-06
+
+
+def _wrap_yards(dim_k, packet, link_axis):
+    finding = jnp.concatenate(tuple((packet for _ in range(lax.psum(1, link_axis)))), dim_k)
+    return lax.all_to_all(finding, link_axis, dim_k, dim_k, tiled=True)
 
 
 def rms_norm(values, gain):
@@ -37,11 +42,7 @@
     factor = 1.0 / math.sqrt(HD)
     normed = rms_norm(tokens, attn_gain)
     joined = jnp.concatenate([w_query, w_keyval], axis=1)
-    head_parts = jnp.dot(
-        lax.all_gather(normed, "req", axis=0, tiled=True),
-        joined,
-        preferred_element_type=jnp.float32,
-    )
+    head_parts = jnp.dot(_wrap_yards(0, normed, "req"), joined, preferred_element_type=jnp.float32)
     query_cols = w_query.shape[1]
     query_part, keyval_part = (
         lax.all_to_all(head_parts[:, :query_cols], "req", split_axis=0, concat_axis=1, tiled=True),

time: 729 us -> 696 us (0.955)
  blocking collectives: 231 us -> 199 us
    all_gather x1 -> x0, blocking collectives: 60.2 us -> none  [body(): lax.all_gather(normed, 'req', axis=0, tiled=True)]
    all_to_all x0 -> x1, blocking collectives: none -> 27.9 us  [_wrap_yards(): return lax.all_to_all(finding, link_axis, dim_k, dim_k, tiled=True)]
where the time goes in v1:
time: 696 us
  waiting for transfers between devices  446 us (64%)
  blocking collectives  199 us (29%)
  between operations  15 us (2%)
  local copies, waits for them, and re-layouts  12.8 us (2%)
  starting transfers between devices  9.49 us (1%)
  other arithmetic  7.09 us (1%)
    unnamed x10, waiting for transfers between devices  296 us
    psum x1, waiting for transfers between devices, body(): ffn_total = lax.psum(ffn_parts, 'ch')  68.9 us
    psum x1, waiting for transfers between devices, body(): summed, own_sum = lax.psum((score_part, own_part), 'ch')  64.5 us
    all_gather x1, blocking collectives, body(): lax.all_gather(normed_two, 'req', axis=0, tiled=True)  59.6 us
    all_gather x1, blocking collectives, body(): lax.all_gather(attn_local, 'req', axis=0, tiled=True)  57 us
    all_to_all x1, blocking collectives, _wrap_yards(): return lax.all_to_all(finding, link_axis, dim_k, dim_k, tiled=True)  27.9 us
    psum x2, blocking collectives, rms_norm(): summed = lax.psum(squares, 'ch')  26.7 us
    all_to_all x1, blocking collectives, body(): lax.all_to_all(out_parts, 'req', split_axis=0, concat_axis=1, tiled=True)  16.1 us
  transfers between devices with their start and end apart: 8, of which 8 were waited for; matrix products, arithmetic and copies ran while one was open for 1% of the time, Pallas kernels for 0%

profile of v1, /device:TPU:1, one launch (start us, length us, event | category | flops | bytes accessed | tf_op | source)
XLA Modules:
  0.0 695.5 jit_solution(11802664696209583861)
XLA Ops:
  7.2 0.9 fusion.36
  8.0 14.7 %psum.35 = f32[2]{0:T(128)S(1)} all-reduce(f32[2]{0:T(128)S(1)} %fusion.36), channel_id=1, replica_groups=mesh['req'=64,'ch'=8] {'ch'}, use_global_device_ids=true, to_apply=%region_1.0 | all-reduce | flops 2 | bytes 16 | tf_op jit(solution)/shard_map/psum | solution.py:21
  22.7 0.8 fusion.38
  23.5 0.5 concatenate.6
  24.0 0.1 all_to_all.50
  24.1 27.9 %all_to_all.69 = bf16[64,2,512]{2,1,0:T(2,128)(2,1)S(1)} all-to-all(bf16[64,2,512]{2,1,0:T(2,128)(2,1)S(1)} %all_to_all.50), channel_id=1, replica_groups=mesh['req'=64,'ch'=8] {'req'}, dimensions={0} | all-to-all | bytes 262144 | tf_op jit(solution)/shard_map/all_to_all | solution.py:15
  52.0 0.1 all_to_all.52
  52.1 1.0 fusion.24
  53.1 0.7 copy.28
  53.8 4.9 all-to-all-start.2
  58.7 0.1 copy.26
  58.8 0.7 reshape.85
  59.5 8.9 %all-to-all-done.2 = f32[64,2,8]{2,1,0:T(2,128)S(1)} async-done(((f32[64,2,8]{2,1,0:T(2,128)}), f32[64,2,8]{2,1,0:T(2,128)S(1)}, u32[]{:S(2)}, u32[]{:S(2)}) %all-to-all-start.2) | async-done | bytes 4128 | tf_op jit(solution)/shard_map/all_to_all | solution.py:49
  68.5 4.4 all-to-all-start.1
  72.9 0.0 reduce-scatter.12.cloned.1.call-start
  72.9 1.2 copy.40
  74.1 0.0 reduce-scatter.12.cloned.1.call-update
  74.1 0.0 reduce-scatter.10.cloned.1.call-start
  74.2 8.1 %all-to-all-done.1 = f32[64,1,128]{2,1,0:T(1,128)S(1)} async-done(((f32[64,1,128]{2,1,0:T(1,128)}), f32[64,1,128]{2,1,0:T(1,128)S(1)}, u32[]{:S(2)}, u32[]{:S(2)}) %all-to-all-start.1) | async-done | bytes 32800 | tf_op jit(solution)/shard_map/all_to_all | solution.py:48
  82.3 0.5 broadcast.73
  82.8 0.7 reduce
  83.5 0.1 reshape.86
  83.7 2.0 copy.39
  85.7 0.0 all-reduce.5.cloned.1.call-start
  85.8 0.1 fusion.35
  85.9 23.1 %reduce-scatter.12.cloned.1.call-done = f32[64,2]{1,0:T(8,128)} async-done(((f32[512,2]{1,0:T(8,128)}), f32[64,2]{1,0:T(8,128)}) %reduce-scatter.12.cloned.1.call-update) | async-done | bytes 528
  109.0 0.8 copy.36
  109.8 47.1 %reduce-scatter.10.cloned.1.call-done = f32[512,2]{1,0:T(8,128)} async-done(((f32[4096,2]{1,0:T(8,128)}), f32[512,2]{1,0:T(8,128)}) %reduce-scatter.10.cloned.1.call-update) | async-done | bytes 4112
  157.0 1.1 copy.34
  158.0 0.1 reshape.71
  158.1 0.9 fusion.3
  159.0 0.0 reduce-scatter.14.cloned.1.call-start
  159.1 0.1 slice_convert_fusion
  159.2 0.1 multiply_reduce_fusion
  159.2 11.8 %psum.37 = f32[2,16]{1,0:T(2,128)S(1)} all-reduce(f32[2,16]{1,0:T(2,128)S(1)} %multiply_reduce_fusion), channel_id=1, replica_groups=mesh['req'=64,'ch'=8] {'ch'}, use_global_device_ids=true, to_apply=%region_7.8 | all-reduce | flops 32 | bytes 256 | tf_op jit(solution)/shard_map/psum | solution.py:65
  171.1 64.5 %all-reduce.5.cloned.1.call-done = f32[2,16,2048]{2,1,0:T(8,128)} async-done(((f32[2,16,2048]{2,1,0:T(8,128)}), f32[2,16,2048]{2,1,0:T(8,128)}) %all-reduce.5.cloned.1.call-update) | async-done | bytes 262160 | tf_op jit(solution)/shard_map/psum | solution.py:65
  235.6 1.1 fusion.7
  236.6 1.2 fusion.8
  237.8 1.2 fusion.1
  239.0 0.1 reshape.73
  239.1 57.0 %all-gather = bf16[64,2,512]{2,1,0:T(2,128)(2,1)S(1)} all-gather(bf16[1,2,512]{2,1,0:T(2,128)(2,1)S(1)} %reshape.73), channel_id=1, replica_groups=mesh['req'=64,'ch'=8] {'req'}, dimensions={0}, use_global_device_ids=true | all-gather | bytes 133120 | tf_op jit(solution)/shard_map/all_gather | solution.py:86
  296.1 0.1 reshape.74
  296.1 0.2 fusion.54
  296.3 0.1 reshape.87
  296.4 16.1 %all_to_all.70 = f32[64,1,128]{2,1,0:T(1,128)S(1)} all-to-all(f32[64,1,128]{2,1,0:T(1,128)S(1)} %reshape.87), channel_id=1, replica_groups=mesh['req'=64,'ch'=8] {'req'}, dimensions={0} | all-to-all | bytes 65536 | tf_op jit(solution)/shard_map/all_to_all | solution.py:90
  312.5 0.7 reduce.1
  313.3 0.1 reshape.88
  313.4 2.0 copy.41
  315.5 0.0 reduce-scatter.14.cloned.1.call-update
  315.5 0.0 all-reduce.7.cloned.1.call-start
  315.5 32.4 %reduce-scatter.14.cloned.1.call-done = f32[512,2]{1,0:T(8,128)} async-done(((f32[4096,2]{1,0:T(8,128)}), f32[512,2]{1,0:T(8,128)}) %reduce-scatter.14.cloned.1.call-update) | async-done | bytes 4112
  348.0 1.1 copy.38
  349.0 0.1 fusion.40
  349.2 12.0 %psum.38 = f32[2]{0:T(128)S(1)} all-reduce(f32[2]{0:T(128)S(1)} %get-tuple-element.2), channel_id=1, replica_groups=mesh['req'=64,'ch'=8] {'ch'}, use_global_device_ids=true, to_apply=%region_11.12 | all-reduce | flops 2 | bytes 16 | tf_op jit(solution)/shard_map/psum | solution.py:21
  361.2 0.1 fusion.44
  361.2 59.6 %all-gather.1 = bf16[64,2,512]{2,1,0:T(2,128)(2,1)S(1)} all-gather(bf16[1,2,512]{2,1,0:T(2,128)(2,1)S(1)} %fusion.44), channel_id=1, replica_groups=mesh['req'=64,'ch'=8] {'req'}, dimensions={0}, use_global_device_ids=true | all-gather | bytes 133120 | tf_op jit(solution)/shard_map/all_gather | solution.py:96
  420.8 0.1 reshape.76
  420.9 0.9 fusion.55
  421.8 0.0 all-reduce.9.cloned.1.call-start
  421.9 68.9 %all-reduce.7.cloned.1.call-done = f32[128,384]{1,0:T(8,128)} async-done(((f32[128,384]{1,0:T(8,128)}), f32[128,384]{1,0:T(8,128)}) %all-reduce.7.cloned.1.call-update) | async-done | bytes 196624 | tf_op jit(solution)/shard_map/psum | solution.py:100
  490.8 1.9 fusion.28
  492.7 1.3 dynamic-slice
  494.6 192.7 %all-reduce.9.cloned.1.call-done = f32[128,512]{1,0:T(8,128)} async-done(((f32[128,512]{1,0:T(8,128)}), f32[128,512]{1,0:T(8,128)}) %all-reduce.9.cloned.1.call-update) | async-done | bytes 262160
  687.4 1.3 fusion.43
  (29 shorter events, 0.2 us)
Async XLA Ops:
  7.2 413.7 %copy-start = (bf16[512,384]{1,0:T(8,128)(2,1)S(1)}, bf16[512,384]{1,0:T(8,128)(2,1)}, u32[]{:S(2)}) copy-start(bf16[512,384]{1,0:T(8,128)(2,1)} %param.20) | copy-start | bytes 1179652
  7.2 67.0 %copy-start.8 = (s32[2]{0:T(128)S(1)}, s32[2]{0:T(128)}, u32[]{:S(2)}) copy-start(s32[2]{0:T(128)} %param.17) | copy-start | bytes 28
  53.8 14.7 %all-to-all-start.2 = ((f32[64,2,8]{2,1,0:T(2,128)}), f32[64,2,8]{2,1,0:T(2,128)S(1)}, u32[]{:S(2)}, u32[]{:S(2)}) async-start(f32[64,2,8]{2,1,0:T(2,128)} %bitcast.3), calls=%async_computation.2 | async-start | bytes 131072 | tf_op jit(solution)/shard_map/all_to_all | solution.py:49
  68.5 13.8 %all-to-all-start.1 = ((f32[64,1,128]{2,1,0:T(1,128)}), f32[64,1,128]{2,1,0:T(1,128)S(1)}, u32[]{:S(2)}, u32[]{:S(2)}) async-start(f32[64,1,128]{2,1,0:T(1,128)} %reshape.85), calls=%async_computation.1 | async-start | bytes 65536 | tf_op jit(solution)/shard_map/all_to_all | solution.py:48
  72.9 36.1 %reduce-scatter.12.cloned.1.call-start = ((), (), s32[]{:S(2)}) async-start(), calls=%async_computation.10 | async-start | bytes 294912
  74.1 82.9 %reduce-scatter.10.cloned.1.call-start = ((), (), s32[]{:S(2)}) async-start(), calls=%async_computation.9 | async-start | bytes 2359296
  83.6 2.1 copy-start.7
  83.6 74.5 %copy-start.2 = (bf16[2,2,32,2048]{3,2,1,0:T(8,128)(2,1)S(1)}, bf16[2,2,32,2048]{3,2,1,0:T(8,128)(2,1)}, u32[]{:S(2)}) copy-start(bf16[2,2,32,2048]{3,2,1,0:T(8,128)(2,1)} %param.15) | copy-start | bytes 1572868
  85.7 210.4 %copy-start.3 = (bf16[512,64]{0,1:T(8,128)(2,1)S(1)}, bf16[512,64]{0,1:T(8,128)(2,1)}, u32[]{:S(2)}) copy-start(bf16[512,64]{0,1:T(8,128)(2,1)} %param.18) | copy-start | bytes 196612
  85.7 149.8 %all-reduce.5.cloned.1.call-start = ((), (), s32[]{:S(2)}) async-start(), calls=%async_computation.7 | async-start | bytes 524288 | tf_op jit(solution)/shard_map/psum | solution.py:65
  109.8 205.6 %copy-start.5 = (bf16[2,64]{1,0:T(2,128)(2,1)}, bf16[2,64]{1,0:T(2,128)(2,1)S(1)}, u32[]{:S(2)}) copy-start(bf16[2,64]{1,0:T(2,128)(2,1)S(1)} %copy.36) | copy-start | bytes 772
  159.0 188.9 %reduce-scatter.14.cloned.1.call-start = ((), (), s32[]{:S(2)}) async-start(), calls=%async_computation.11 | async-start | bytes 2359296
  313.4 35.6 %copy-start.4 = (bf16[2,512]{1,0:T(2,128)(2,1)S(1)}, bf16[2,512]{1,0:T(2,128)(2,1)}, u32[]{:S(2)}) copy-start(bf16[2,512]{1,0:T(2,128)(2,1)} %param.11) | copy-start | bytes 6148
  313.4 47.8 %copy-start.6 = (f32[512]{0:T(512)S(1)}, f32[512]{0:T(512)}, u32[]{:S(2)}) copy-start(f32[512]{0:T(512)} %param.19) | copy-start | bytes 6148
  315.5 175.3 %copy-start.1 = (bf16[192,512]{1,0:T(8,128)(2,1)S(1)}, bf16[192,512]{1,0:T(8,128)(2,1)}, u32[]{:S(2)}) copy-start(bf16[192,512]{1,0:T(8,128)(2,1)} %param.21) | copy-start | bytes 589828
  315.5 175.3 %all-reduce.7.cloned.1.call-start = ((), (), s32[]{:S(2)}) async-start(), calls=%async_computation.8 | async-start | bytes 393216 | tf_op jit(solution)/shard_map/psum | solution.py:100
  421.8 265.6 %all-reduce.9.cloned.1.call-start = ((), (), s32[]{:S(2)}) async-start(), calls=%async_computation.12 | async-start | bytes 524288
Sparse Core Ops, SparseCore 0:
  76.5 32.4 reduce-scatter.11
  111.8 45.0 reduce-scatter.9
  159.3 76.2 all-reduce.4
  315.6 32.3 reduce-scatter.13
  421.9 68.8 all-reduce.6
  494.1 193.2 all-reduce.8
